TPU v7x, 256 devices: a whole 4x4x8 slice. The times are simulated.
256 devices in a mesh: dp: 64 (over y, z, core), seq: 4 (over x).
Axes of the slice: x: 4, y: 4, z: 8, core: 2. Of those that a mesh axis runs over, the one named last changes fastest.
Arguments:
- frames: bfloat16 [32768, 1536], P('dp', 'seq')
- owner_slot: int32 [32768], P('dp'), may hold values from -1 to 32767, as said below
- segment: int32 [64, 512], P('dp'), may hold values from 0 to 2, never falling along the last dimension, each value on 1 to 256 neighbouring positions
- norm_gain: float32 [1536], replicated, may hold values from 0.25 to 1.75
- expand: bfloat16 [1536, 2, 1536], P('dp', None, 'seq'), may hold values from -0.15625 to 0.15625
- kernel: float32 [9, 1536], P(None, 'seq'), may hold values from -2.5 to 2.5
- project: bfloat16 [1536, 1536], P('seq', 'dp'), may hold values from -0.15625 to 0.15625
- cotangent: bfloat16 [32768, 1536], P('dp', 'seq'), may hold values from -6 to 6
Outputs:
- output: bfloat16 [32768, 1536], P('dp', 'seq')
- grad_frames: bfloat16 [32768, 1536], P('dp', 'seq')
- grad_gain: float32 [1536], P('seq')
- grad_kernel: float32 [9, 1536], P(None, 'seq')
- grad_expand: float32 [1536, 2, 1536], P('dp', None, 'seq')
- grad_project: float32 [1536, 1536], P('seq', 'dp')
Inputs may be any that keep to these rules, and one draw needn't show every extreme that they name: `owner_slot`: for each arrival row, the balanced row that takes it, or -1 for an empty arrival row; no balanced row is named twice. The live rows of each pack come first, contiguous, ordered by sending index of dp and then by arrival row; empty rows fill the pack's tail. Of the 512 arrival rows of one index of dp, at most 8 name rows of any one pack; some pack takes exactly 8 rows from every index of dp. `segment`: within each pack the utterance numbers never fall; a pack holds 3 utterances of 1 to 256 frames, one of exactly 256.
All inputs are finite; a program needn't handle non-finite values.
Results may differ from a plain program's by a relative error of at most 0.01.
Values may be sent and summed in bfloat16 or wider, within the bound.
No kernel may reach another device: no remote copies, remote signals or barrier semaphores. Data moves between devices by JAX's collectives and lax.ppermute only.
A program may use at most 128 MiB of HBM per device.

v0:
```python
import math
import jax
import jax.numpy as jnp
from jax import lax
from jax.sharding import PartitionSpec as P

D = 1536
KSIZE = 9
EPS = 1e-05


def conv_masks(labels):
    half_width = (KSIZE - 1) // 2
    length = labels.shape[0]
    padded = jnp.pad(labels, (half_width, half_width), constant_values=-1)
    return [
        (padded[tap_index : tap_index + length] == labels).astype(jnp.float32)[:, None]
        for tap_index in range(KSIZE)
    ]


def depthwise(signal, kernel, tap_masks):
    half_width = (KSIZE - 1) // 2
    length = signal.shape[0]
    padded = jnp.pad(signal, ((half_width, half_width), (0, 0)))
    total = jnp.zeros(signal.shape, jnp.float32)
    for tap_index in range(KSIZE):
        total = (
            total
            + kernel[tap_index] * padded[tap_index : tap_index + length] * tap_masks[tap_index]
        )
    return total


def depthwise_back(signal, upstream, kernel, tap_masks):
    half_width = (KSIZE - 1) // 2
    length = signal.shape[0]
    padded = jnp.pad(signal, ((half_width, half_width), (0, 0)))
    spread = jnp.zeros((length + 2 * half_width, signal.shape[1]), jnp.float32)
    tap_sums = []
    for tap_index in range(KSIZE):
        masked = upstream * tap_masks[tap_index]
        tap_sums.append(jnp.sum(masked * padded[tap_index : tap_index + length], axis=0))
        spread = spread + jnp.pad(
            kernel[tap_index] * masked, ((tap_index, 2 * half_width - tap_index), (0, 0))
        )
    return (jnp.stack(tap_sums), spread[half_width : half_width + length])


def place_rows(incoming, landing, row_count):
    flat = incoming.reshape(-1, incoming.shape[-1])
    total_slots = flat.shape[0]
    inverse = (
        jnp.full((row_count + 1,), total_slots, jnp.int32)
        .at[landing.reshape(-1)]
        .set(jnp.arange(total_slots, dtype=jnp.int32))[:row_count]
    )
    padded = jnp.concatenate([flat, jnp.zeros((1, flat.shape[1]), flat.dtype)])
    return (padded[inverse], inverse < total_slots)


def shards(frames, owner_slot, segment, norm_gain, expand, kernel, project, cotangent):
    row_count, quarter = frames.shape
    groups = lax.axis_size("dp")
    lane_index = lax.axis_index("seq")
    capacity = row_count // groups
    bucket_slots = groups * capacity
    dest_group = jnp.where(owner_slot >= 0, owner_slot // row_count, groups)
    onehot = (dest_group[:, None] == jnp.arange(groups, dtype=jnp.int32)[None, :]).astype(jnp.int32)
    earlier = jnp.cumsum(onehot, axis=0) - onehot
    within = jnp.sum(earlier * onehot, axis=1)
    send_pos = jnp.where(owner_slot >= 0, dest_group * capacity + within, bucket_slots)
    source_row = (
        jnp.full((bucket_slots + 1,), row_count, jnp.int32)
        .at[send_pos]
        .set(jnp.arange(row_count, dtype=jnp.int32))[:bucket_slots]
    )
    slot_padded = jnp.concatenate([owner_slot, jnp.full((1,), -1, jnp.int32)])
    named_slot = slot_padded[source_row]
    landing_out = jnp.where(named_slot >= 0, named_slot % row_count, row_count).reshape(
        groups, capacity
    )
    padded_in = jnp.concatenate([frames, jnp.zeros((1, quarter), jnp.bfloat16)])
    outgoing = padded_in[source_row].reshape(groups, capacity, quarter)
    incoming, landing = (
        lax.all_to_all(outgoing, "dp", split_axis=0, concat_axis=0, tiled=True),
        lax.all_to_all(landing_out, "dp", split_axis=0, concat_axis=0, tiled=True),
    )
    local_rows, occupied = place_rows(incoming, landing, row_count)
    whole_rows = lax.all_gather(local_rows, "seq", axis=1, tiled=True)
    live_col = occupied.astype(jnp.float32)[:, None]
    floats = whole_rows.astype(jnp.float32)
    row_mean = jnp.mean(floats, axis=1, keepdims=True)
    centred = floats - row_mean
    inv_scale = lax.rsqrt(jnp.mean(centred * centred, axis=1, keepdims=True) + EPS)
    normed = centred * inv_scale
    scaled = (normed * norm_gain).astype(jnp.bfloat16)
    expand_full = lax.all_gather(expand, "dp", axis=0, tiled=True).reshape(D, 2 * quarter)
    project_full = lax.all_gather(project, "dp", axis=1, tiled=True)
    joined = jnp.dot(scaled, expand_full, preferred_element_type=jnp.float32)
    value_half = joined[:, :quarter]
    gate_sig = jax.nn.sigmoid(joined[:, quarter:])
    glu_out = value_half * gate_sig
    tap_masks = conv_masks(segment[0])
    conv_out = depthwise(glu_out, kernel, tap_masks)
    conv_sig = jax.nn.sigmoid(conv_out)
    hidden = (conv_out * conv_sig * live_col).astype(jnp.bfloat16)
    partial_out = jnp.dot(hidden, project_full, preferred_element_type=jnp.float32)
    mixed_share = lax.psum_scatter(
        partial_out.astype(jnp.bfloat16), "seq", scatter_dimension=1, tiled=True
    ).astype(jnp.float32)
    output = (local_rows.astype(jnp.float32) + mixed_share).astype(jnp.bfloat16)
    inv_root = 1.0 / math.sqrt(row_count * groups)
    cot_full = lax.all_gather(cotangent, "seq", axis=1, tiled=True)
    project_term = lax.dot_general(
        hidden, cot_full, (((0,), (0,)), ((), ())), preferred_element_type=jnp.float32
    )
    grad_project = lax.psum_scatter(project_term, "dp", scatter_dimension=1, tiled=True) * inv_root
    hidden_grad = (
        lax.dot_general(
            cot_full, project_full, (((1,), (1,)), ((), ())), preferred_element_type=jnp.float32
        )
        * live_col
    )
    conv_grad = hidden_grad * (conv_sig + conv_out * conv_sig * (1.0 - conv_sig))
    kernel_term, glu_grad = depthwise_back(glu_out, conv_grad, kernel, tap_masks)
    proj_grad = jnp.concatenate(
        [glu_grad * gate_sig, glu_grad * value_half * gate_sig * (1.0 - gate_sig)], axis=1
    ).astype(jnp.bfloat16)
    term_block = lax.dot_general(
        scaled, proj_grad, (((0,), (0,)), ((), ())), preferred_element_type=jnp.float32
    )
    grad_expand = (
        lax.psum_scatter(
            term_block.reshape(expand.shape[0] * lax.axis_size("dp"), 2, quarter),
            "dp",
            scatter_dimension=0,
            tiled=True,
        )
        * inv_root
    )
    scaled_part = lax.dot_general(
        proj_grad, expand_full, (((1,), (1,)), ((), ())), preferred_element_type=jnp.float32
    )
    normed_local = lax.dynamic_slice_in_dim(normed, lane_index * quarter, quarter, 1)
    scaled_grad = lax.psum(scaled_part.astype(jnp.bfloat16), "seq").astype(jnp.float32)
    normed_grad = scaled_grad * norm_gain
    first_mean = jnp.mean(normed_grad, axis=1, keepdims=True)
    second_mean = jnp.mean(normed_grad * normed, axis=1, keepdims=True)
    full_grad = inv_scale * (normed_grad - first_mean - normed * second_mean)
    packed_grad = lax.dynamic_slice_in_dim(full_grad, lane_index * quarter, quarter, 1)
    scaled_share = lax.dynamic_slice_in_dim(scaled_grad, lane_index * quarter, quarter, 1)
    gain_term = jnp.sum(scaled_share * normed_local, axis=0)
    gain_sum, kernel_sum = lax.psum((gain_term, kernel_term), "dp")
    back_rows = (packed_grad + cotangent.astype(jnp.float32)).astype(jnp.bfloat16)
    back_padded = jnp.concatenate([back_rows, jnp.zeros((1, quarter), jnp.bfloat16)])
    returning = back_padded[landing.reshape(-1)].reshape(groups, capacity, quarter)
    returned = lax.all_to_all(returning, "dp", split_axis=0, concat_axis=0, tiled=True)
    returned_flat = jnp.concatenate(
        [returned.reshape(bucket_slots, quarter), jnp.zeros((1, quarter), jnp.bfloat16)]
    )
    grad_frames = returned_flat[send_pos]
    return (
        output,
        grad_frames,
        gain_sum * inv_root,
        kernel_sum * inv_root,
        grad_expand,
        grad_project,
    )


def solution(mesh):
    placed = (
        P("dp", "seq"),
        P("dp"),
        P("dp", None),
        P(),
        P("dp", None, "seq"),
        P(None, "seq"),
        P("seq", "dp"),
        P("dp", "seq"),
    )
    return jax.shard_map(
        shards,
        mesh=mesh,
        in_specs=placed,
        out_specs=(
            P("dp", "seq"),
            P("dp", "seq"),
            P("seq"),
            P(None, "seq"),
            P("dp", None, "seq"),
            P("seq", "dp"),
        ),
        check_vma=False,
    )
```

profile of v0, /device:TPU:4, one launch (start us, length us, event | category | flops | bytes accessed | tf_op | source)
XLA Modules:
  0.0 722.8 jit_solution(6718990988851698500)
XLA Ops:
  7.2 0.7 fusion.22
  7.9 0.7 fusion.55
  8.6 1.2 reduce-window.6
  9.8 0.2 slice_reduce_fusion
  10.2 0.7 compare_select_fusion.3
  10.9 2.4 scatter_custom_fusion
  13.4 0.7 pad_add_fusion.7
  14.1 2.3 gather_fusion.1
  16.5 0.6 fusion.20
  17.1 12.1 %all-to-all-start.1 = ((s32[64,1,8]{2,1,0:T(1,128)}), s32[64,1,8]{2,1,0:T(1,128)S(1)}, u32[]{:S(2)}, u32[]{:S(2)}) async-start(s32[64,1,8]{2,1,0:T(1,128)} %bitcast.4), calls=%async_computation.1 | async-start | bytes 65536 | tf_op jit(solution)/shard_map/all_to_all | solution.py:87
  29.3 2.6 gather_fusion
  31.9 6.8 all-to-all-done.1
  38.7 4.6 all-to-all-start
  43.4 0.5 broadcast.267
  43.9 0.7 reduce.23
  44.8 2.4 scatter_custom_fusion.1
  47.2 10.6 %all-to-all-done = bf16[64,8,384]{2,1,0:T(8,128)(2,1)S(1)} async-done(((bf16[64,8,384]{2,1,0:T(8,128)(2,1)}), bf16[64,8,384]{2,1,0:T(8,128)(2,1)S(1)}, u32[]{:S(2)}, u32[]{:S(2)}) %all-to-all-start) | async-done | bytes 393248 | tf_op jit(solution)/shard_map/all_to_all | solution.py:86
  57.9 2.6 gather_fusion.2
  60.6 0.7 all-gather.6.cloned.1.call-update
  61.3 0.7 all-gather.8.cloned.1.call-update
  62.0 0.5 all-gather.10.cloned.1.call-update
  62.6 0.2 all-reduce.21.cloned.1.call-start
  63.0 22.6 %all-gather.12.cloned.1.call-done = bf16[512,1536]{1,0:T(8,128)(2,1)} async-done(((bf16[512,384]{1,0:T(8,128)(2,1)}), bf16[512,1536]{1,0:T(8,128)(2,1)}) %all-gather.12.cloned.1.call-update) | async-done | bytes 1572880 | tf_op jit(solution)/shard_map/all_gather | solution.py:90
  85.6 1.8 convert_reduce_fusion
  87.4 0.5 fusion.2
  88.0 79.3 %all-gather.6.cloned.1.call-done = bf16[1536,2,384]{2,1,0:T(2,128)(2,1)} async-done(((bf16[24,2,384]{2,1,0:T(2,128)(2,1)}), bf16[1536,2,384]{2,1,0:T(2,128)(2,1)}) %all-gather.6.cloned.1.call-update) | async-done | bytes 2359312 | tf_op jit(solution)/shard_map/all_gather | solution.py:98
  167.3 2.1 copy.23
  169.5 1.5 fusion.13
  171.0 0.2 slice_multiply_fusion
  171.2 0.9 copy-done.3
  172.1 2.0 multiply_add_fusion
  174.1 70.2 %all-gather.8.cloned.1.call-done = bf16[384,1536]{0,1:T(8,128)(2,1)} async-done(((bf16[384,24]{0,1:T(8,128)(2,1)}), bf16[384,1536]{0,1:T(8,128)(2,1)}) %all-gather.8.cloned.1.call-update) | async-done | bytes 1179664 | tf_op jit(solution)/shard_map/all_gather | solution.py:99
  244.4 27.2 %all-gather.10.cloned.1.call-done = bf16[512,1536]{1,0:T(8,128)(2,1)} async-done(((bf16[512,384]{1,0:T(8,128)(2,1)}), bf16[512,1536]{1,0:T(8,128)(2,1)}) %all-gather.10.cloned.1.call-update) | async-done | bytes 1572880 | tf_op jit(solution)/shard_map/all_gather | solution.py:114
  271.6 7.9 %multiply_reduce_fusion.1 = (f32[384]{0:T(512)}, f32[384]{0:T(512)}, f32[384]{0:T(512)}, f32[384]{0:T(512)}, f32[384]{0:T(512)}, /*index=5*/f32[384]{0:T(512)}, ...) fusion(f32[512,384]{1,0:T(8,128)} %copy-done.3, ...), kind=kOutput, calls=%fused_computation.36 | convolution fusion | flops 611054208 | bytes 5932032 | tf_op jit(solution)/shard_map/dot_general | solution.py:120
  279.5 0.7 multiply_multiply_fusion.7
  280.4 0.6 multiply_convert_fusion.2
  281.0 0.2 multiply_convert_fusion.1
  281.3 0.7 copy-done.8
  282.0 0.8 copy-done.5
  282.8 2.6 convolution_convert_fusion
  285.5 4.8 fusion.12
  290.3 8.2 %copy.19 = f32[1536,2,384]{2,1,0:T(2,128)} copy(f32[1536,2,384]{0,2,1:T(8,128)} %bitcast.41) | data formatting | bytes 9437184 | tf_op jit(solution)/shard_map/reshape | solution.py:135
  298.5 0.6 copy-done.26
  299.1 2.6 convolution_convert_fusion.1
  301.7 1.6 copy.20
  303.3 0.3 reduce-scatter.9.cloned.1.call-start
  303.5 4.2 fusion.46
  307.7 0.6 copy-done.13
  308.4 32.9 %all-reduce.21.cloned.1.call-done = bf16[512,1536]{1,0:T(8,128)(2,1)} async-done(((bf16[512,1536]{1,0:T(8,128)(2,1)}), bf16[512,1536]{1,0:T(8,128)(2,1)}) %all-reduce.21.cloned.1.call-update) | async-done | bytes 1572880 | tf_op jit(solution)/shard_map/psum | solution.py:146
  341.3 1.9 convert_element_type.110
  343.2 1.1 fusion.11
  344.3 0.4 multiply_reduce_fusion.10
  344.8 2.6 gather_fusion.3
  347.4 10.5 %all-to-all-start.2 = ((bf16[64,8,384]{2,1,0:T(8,128)(2,1)}), bf16[64,8,384]{2,1,0:T(8,128)(2,1)S(1)}, u32[]{:S(2)}, u32[]{:S(2)}) async-start(bf16[64,8,384]{2,1,0:T(8,128)(2,1)} %bitcast.7), calls=%async_computation.2 | async-start | bytes 786432 | tf_op jit(solution)/shard_map/all_to_all | solution.py:158
  357.9 0.6 dynamic-slice
  359.4 251.8 %all-reduce.17 = (f32[384]{0:T(512)S(1)}, f32[9,384]{1,0:T(8,128)S(1)}) all-reduce(f32[384]{0:T(512)S(1)} %get-tuple-element.30, f32[9,384]{1,0:T(8,128)S(1)} %stack.39), channel_id=1, replica_groups=mesh['dp'=64,'seq'=4] {'dp'}, use_global_device_ids=true, to_apply=%region_12.13 | all-reduce | flops 3840 | bytes 30720 | tf_op jit(solution)/shard_map/psum | solution.py:154
  611.2 0.6 broadcast_multiply_fusion.4
  611.8 0.6 broadcast_multiply_fusion.3
  612.4 2.6 gather_fusion.4
  615.0 1.6 dynamic-slice_multiply_fusion
  616.6 1.2 copy.21
  617.8 0.8 add_convert_fusion
  618.6 95.9 %reduce-scatter.9.cloned.1.call-done = f32[384,24]{0,1:T(8,128)} async-done(((f32[384,1536]{0,1:T(8,128)}), f32[384,24]{0,1:T(8,128)}) %reduce-scatter.9.cloned.1.call-update) | async-done | bytes 36880
  714.6 1.4 broadcast_multiply_fusion.2
  (101 shorter events, 1.5 us)
Async XLA Ops:
  7.2 22.1 %copy-start.7 = (bf16[512,384]{1,0:T(8,128)(2,1)S(1)}, bf16[512,384]{1,0:T(8,128)(2,1)}, u32[]{:S(2)}) copy-start(bf16[512,384]{1,0:T(8,128)(2,1)} %param.8) | copy-start | bytes 1179652
  10.9 3.2 copy-start.10
  17.1 21.6 %all-to-all-start.1 = ((s32[64,1,8]{2,1,0:T(1,128)}), s32[64,1,8]{2,1,0:T(1,128)S(1)}, u32[]{:S(2)}, u32[]{:S(2)}) async-start(s32[64,1,8]{2,1,0:T(1,128)} %bitcast.4), calls=%async_computation.1 | async-start | bytes 65536 | tf_op jit(solution)/shard_map/all_to_all | solution.py:87
  38.7 19.1 %all-to-all-start = ((bf16[64,8,384]{2,1,0:T(8,128)(2,1)}), bf16[64,8,384]{2,1,0:T(8,128)(2,1)S(1)}, u32[]{:S(2)}, u32[]{:S(2)}) async-start(bf16[64,8,384]{2,1,0:T(8,128)(2,1)} %bitcast.2), calls=%async_computation | async-start | bytes 786432 | tf_op jit(solution)/shard_map/all_to_all | solution.py:86
  43.3 42.2 %all-gather.12.cloned.1.call-start = ((), (), s32[]{:S(2)}) async-start(), calls=%async_computation.9 | async-start | bytes 1966080 | tf_op jit(solution)/shard_map/all_gather | solution.py:90
  44.7 13.1 %copy-start.12 = (s32[512,1]{0,1:T(1,128)}, s32[512,1]{0,1:T(1,128)S(1)}, u32[]{:S(2)}) copy-start(s32[512,1]{0,1:T(1,128)S(1)} %compare_select_fusion) | copy-start | bytes 6148
  57.9 4.9 copy-start.14
  57.9 5.0 copy-start.15
  60.5 106.8 %all-gather.6.cloned.1.call-start = ((), (), s32[]{:S(2)}) async-start(), calls=%async_computation.5 | async-start | bytes 2396160 | tf_op jit(solution)/shard_map/all_gather | solution.py:98
  61.3 183.1 %all-gather.8.cloned.1.call-start = ((), (), s32[]{:S(2)}) async-start(), calls=%async_computation.6 | async-start | bytes 1198080 | tf_op jit(solution)/shard_map/all_gather | solution.py:99
  62.0 209.6 %all-gather.10.cloned.1.call-start = ((), (), s32[]{:S(2)}) async-start(), calls=%async_computation.7 | async-start | bytes 1966080 | tf_op jit(solution)/shard_map/all_gather | solution.py:114
  62.6 278.7 %all-reduce.21.cloned.1.call-start = ((), (), s32[]{:S(2)}) async-start(), calls=%async_computation.8 | async-start | bytes 3145728 | tf_op jit(solution)/shard_map/psum | solution.py:146
  63.0 208.7 %copy-start.25 = (f32[512]{0:T(512)}, f32[512]{0:T(512)S(1)}, u32[]{:S(2)}) copy-start(f32[512]{0:T(512)S(1)} %compare_convert_fusion) | copy-start | bytes 6148
  85.6 1.9 copy-start
  167.3 2.2 copy-start.9
  169.5 1.5 copy-start.4
  171.2 0.9 copy-start.3
  281.0 1.8 copy-start.5
  281.3 0.7 copy-start.8
  285.5 329.6 %all-reduce.23.cloned.1.call-start = ((), (), s32[]{:S(2)}) async-start(), calls=%async_computation.11 | async-start | bytes 9437184
  298.4 0.7 copy-start.26
  298.4 318.1 %reduce-scatter.7.cloned.1.call-start = ((), (), s32[]{:S(2)}) async-start(), calls=%async_computation.10 | async-start | bytes 1966080
  303.3 411.3 %reduce-scatter.9.cloned.1.call-start = ((), (), s32[]{:S(2)}) async-start(), calls=%async_computation.12 | async-start | bytes 2396160
  307.7 0.7 copy-start.13
  341.3 1.9 copy-start.1
  343.2 1.1 copy-start.6
  344.7 13.2 %copy-start.27 = (u32[256]{0:T(256)S(1)}, u32[256]{0:T(256)}, u32[]{:S(2)}) copy-start(u32[256]{0:T(256)} %constant.110) | copy-start | bytes 3076
  344.7 14.4 %copy-start.11 = (s32[512]{0:T(512)S(1)}, s32[512]{0:T(512)}, u32[]{:S(2)}) copy-start(s32[512]{0:T(512)} %copy-done.10) | copy-start | bytes 6148
  344.7 14.4 %copy-start.24 = (f32[384]{0:T(512)S(1)}, f32[384]{0:T(512)}, u32[]{:S(2)}) copy-start(f32[384]{0:T(512)} %get-tuple-element.9) | copy-start | bytes 4612
  344.8 14.4 %copy-start.23 = (f32[384]{0:T(512)S(1)}, f32[384]{0:T(512)}, u32[]{:S(2)}) copy-start(f32[384]{0:T(512)} %get-tuple-element.10) | copy-start | bytes 4612
  344.8 14.4 %copy-start.22 = (f32[384]{0:T(512)S(1)}, f32[384]{0:T(512)}, u32[]{:S(2)}) copy-start(f32[384]{0:T(512)} %get-tuple-element.11) | copy-start | bytes 4612
  344.8 14.5 %copy-start.21 = (f32[384]{0:T(512)S(1)}, f32[384]{0:T(512)}, u32[]{:S(2)}) copy-start(f32[384]{0:T(512)} %get-tuple-element.12) | copy-start | bytes 4612
  344.8 14.5 %copy-start.20 = (f32[384]{0:T(512)S(1)}, f32[384]{0:T(512)}, u32[]{:S(2)}) copy-start(f32[384]{0:T(512)} %get-tuple-element.16) | copy-start | bytes 4612
  344.8 14.5 %copy-start.19 = (f32[384]{0:T(512)S(1)}, f32[384]{0:T(512)}, u32[]{:S(2)}) copy-start(f32[384]{0:T(512)} %get-tuple-element.13) | copy-start | bytes 4612
  344.8 14.5 %copy-start.18 = (f32[384]{0:T(512)S(1)}, f32[384]{0:T(512)}, u32[]{:S(2)}) copy-start(f32[384]{0:T(512)} %get-tuple-element.14) | copy-start | bytes 4612
  344.8 14.5 %copy-start.17 = (f32[384]{0:T(512)S(1)}, f32[384]{0:T(512)}, u32[]{:S(2)}) copy-start(f32[384]{0:T(512)} %get-tuple-element.15) | copy-start | bytes 4612
  344.8 14.5 %copy-start.16 = (f32[384]{0:T(512)S(1)}, f32[384]{0:T(512)}, u32[]{:S(2)}) copy-start(f32[384]{0:T(512)} %get-tuple-element.8) | copy-start | bytes 4612
  347.4 265.0 %all-to-all-start.2 = ((bf16[64,8,384]{2,1,0:T(8,128)(2,1)}), bf16[64,8,384]{2,1,0:T(8,128)(2,1)S(1)}, u32[]{:S(2)}, u32[]{:S(2)}) async-start(bf16[64,8,384]{2,1,0:T(8,128)(2,1)} %bitcast.7), calls=%async_computation.2 | async-start | bytes 786432 | tf_op jit(solution)/shard_map/all_to_all | solution.py:158
  612.4 5.4 copy-start.2
Sparse Core Ops, SparseCore 0:
  60.6 24.8 all-gather.11
  88.2 79.0 all-gather.5
  170.0 74.3 all-gather.7
  246.1 25.4 all-gather.9
  285.6 55.6 all-reduce.20
  344.7 201.8 all-reduce.22
  549.1 25.4 reduce-scatter.6
  578.7 135.7 reduce-scatter.8
where the time goes:
time: 724 us; the launch traced here: 723 us
  waiting for transfers between devices  348 us (48%)
  blocking collectives  252 us (35%)
  local copies, waits for them, and re-layouts  36.2 us (5%)
  starting transfers between devices  27.9 us (4%)
  matrix products  23.5 us (3%)
  other arithmetic  20.3 us (3%)
  between operations  15.4 us (2%)
    psum x1, blocking collectives, shards(): gain_sum, kernel_sum = lax.psum((gain_term, kernel_term), 'dp')  252 us
    unnamed x11, waiting for transfers between devices  97.9 us
    all_gather x1, waiting for transfers between devices, shards(): lax.all_gather(expand, 'dp', axis=0, tiled=True).reshape(D, 2 * quarter)  79.3 us
    all_gather x1, waiting for transfers between devices, shards(): project_full = lax.all_gather(project, 'dp', axis=1, tiled=True)  70.2 us
    psum x1, waiting for transfers between devices, shards(): lax.psum(scaled_part.astype(jnp.bfloat16), 'seq').astype(jnp.float32)  32.9 us
    all_gather x1, waiting for transfers between devices, shards(): cot_full = lax.all_gather(cotangent, 'seq', axis=1, tiled=True)  27.2 us
    all_gather x1, waiting for transfers between devices, shards(): whole_rows = lax.all_gather(local_rows, 'seq', axis=1, tiled=True)  22.6 us
  transfers between devices with their start and end apart: 11, of which 8 were waited for; matrix products, arithmetic and copies ran while one was open for 7% of the time, Pallas kernels for 0%

commit v1 on v0

--- a/solution.py
+++ b/solution.py
@@ -7,6 +7,10 @@
 D = 1536
 KSIZE = 9
 EPS = 1e-05
+
+
+def arrange_the_frame(buf, named_axis):
+    return jnp.sum(jax.lax.all_gather(buf, named_axis), 0)
 
 
 def conv_masks(labels):
@@ -143,7 +147,7 @@
         proj_grad, expand_full, (((1,), (1,)), ((), ())), preferred_element_type=jnp.float32
     )
     normed_local = lax.dynamic_slice_in_dim(normed, lane_index * quarter, quarter, 1)
-    scaled_grad = lax.psum(scaled_part.astype(jnp.bfloat16), "seq").astype(jnp.float32)
+    scaled_grad = arrange_the_frame(scaled_part.astype(jnp.bfloat16), "seq").astype(jnp.float32)
     normed_grad = scaled_grad * norm_gain
     first_mean = jnp.mean(normed_grad, axis=1, keepdims=True)
     second_mean = jnp.mean(normed_grad * normed, axis=1, keepdims=True)

time: 724 us -> 990 us (1.37)
  waiting for transfers between devices: 348 us -> 615 us
    unnamed x11, waiting for transfers between devices: 97.9 us -> 329 us
    all_gather x0 -> x1, waiting for transfers between devices: none -> 69.5 us  [arrange_the_frame(): return jnp.sum(jax.lax.all_gather(buf, named_axis), 0)]
    psum x1 -> x0, waiting for transfers between devices: 32.9 us -> none  [shards(): lax.psum(scaled_part.astype(jnp.bfloat16), 'seq').astype(jnp.float32)]
  transfers between devices with their start and end apart: 11 -> 11, of which waited for: 8 -> 10; matrix products, arithmetic and copies ran while one was open for 7% -> 5% of each run, Pallas kernels for 0% -> 0%
where the time goes in v1:
time: 990 us; the launch traced here: 989 us
  waiting for transfers between devices  615 us (62%)
  blocking collectives  246 us (25%)
  local copies, waits for them, and re-layouts  36.1 us (4%)
  starting transfers between devices  27.9 us (3%)
  matrix products  24.5 us (2%)
  other arithmetic  23.5 us (2%)
  between operations  15.4 us (2%)
    unnamed x11, waiting for transfers between devices  329 us
    psum x1, blocking collectives, shards(): gain_sum, kernel_sum = lax.psum((gain_term, kernel_term), 'dp')  246 us
    all_gather x1, waiting for transfers between devices, shards(): lax.all_gather(expand, 'dp', axis=0, tiled=True).reshape(D, 2 * quarter)  79.3 us
    all_gather x1, waiting for transfers between devices, shards(): project_full = lax.all_gather(project, 'dp', axis=1, tiled=True)  70.2 us
    all_gather x1, waiting for transfers between devices, arrange_the_frame(): return jnp.sum(jax.lax.all_gather(buf, named_axis), 0)  69.5 us
    all_gather x1, waiting for transfers between devices, shards(): cot_full = lax.all_gather(cotangent, 'seq', axis=1, tiled=True)  27.2 us
    all_gather x1, waiting for transfers between devices, shards(): whole_rows = lax.all_gather(local_rows, 'seq', axis=1, tiled=True)  22.6 us
  transfers between devices with their start and end apart: 11, of which 10 were waited for; matrix products, arithmetic and copies ran while one was open for 5% of the time, Pallas kernels for 0%

profile of v1, /device:TPU:4, one launch (start us, length us, event | category | flops | bytes accessed | tf_op | source)
XLA Modules:
  0.0 988.8 jit_solution(17328579810417582964)
XLA Ops:
  7.2 0.7 fusion.22
  7.9 0.7 fusion.55
  8.6 1.2 reduce-window.6
  10.2 0.7 compare_select_fusion.3
  10.9 2.4 scatter_custom_fusion
  13.4 0.7 pad_add_fusion.7
  14.1 2.3 gather_fusion.1
  16.5 0.6 fusion.20
  17.1 12.1 %all-to-all-start.1 = ((s32[64,1,8]{2,1,0:T(1,128)}), s32[64,1,8]{2,1,0:T(1,128)S(1)}, u32[]{:S(2)}, u32[]{:S(2)}) async-start(s32[64,1,8]{2,1,0:T(1,128)} %bitcast.4), calls=%async_computation.1 | async-start | bytes 65536 | tf_op jit(solution)/shard_map/all_to_all | solution.py:91
  29.3 2.6 gather_fusion
  31.9 6.8 all-to-all-done.1
  38.7 4.6 all-to-all-start
  43.4 0.5 broadcast.267
  43.9 0.7 reduce.24
  44.8 2.4 scatter_custom_fusion.1
  47.2 10.6 %all-to-all-done = bf16[64,8,384]{2,1,0:T(8,128)(2,1)S(1)} async-done(((bf16[64,8,384]{2,1,0:T(8,128)(2,1)}), bf16[64,8,384]{2,1,0:T(8,128)(2,1)S(1)}, u32[]{:S(2)}, u32[]{:S(2)}) %all-to-all-start) | async-done | bytes 393248 | tf_op jit(solution)/shard_map/all_to_all | solution.py:90
  57.9 2.6 gather_fusion.2
  60.6 0.7 all-gather.8.cloned.1.call-update
  61.3 0.7 all-gather.10.cloned.1.call-update
  62.0 0.5 all-gather.12.cloned.1.call-update
  63.0 22.6 %all-gather.14.cloned.1.call-done = bf16[512,1536]{1,0:T(8,128)(2,1)} async-done(((bf16[512,384]{1,0:T(8,128)(2,1)}), bf16[512,1536]{1,0:T(8,128)(2,1)}) %all-gather.14.cloned.1.call-update) | async-done | bytes 1572880 | tf_op jit(solution)/shard_map/all_gather | solution.py:94
  85.6 1.8 convert_reduce_fusion
  87.4 0.5 fusion.2
  88.0 79.3 %all-gather.8.cloned.1.call-done = bf16[1536,2,384]{2,1,0:T(2,128)(2,1)} async-done(((bf16[24,2,384]{2,1,0:T(2,128)(2,1)}), bf16[1536,2,384]{2,1,0:T(2,128)(2,1)}) %all-gather.8.cloned.1.call-update) | async-done | bytes 2359312 | tf_op jit(solution)/shard_map/all_gather | solution.py:102
  167.3 2.1 copy.23
  169.5 1.5 fusion.13
  171.2 0.9 copy-done.2
  172.1 2.0 multiply_add_fusion
  174.2 70.2 %all-gather.10.cloned.1.call-done = bf16[384,1536]{0,1:T(8,128)(2,1)} async-done(((bf16[384,24]{0,1:T(8,128)(2,1)}), bf16[384,1536]{0,1:T(8,128)(2,1)}) %all-gather.10.cloned.1.call-update) | async-done | bytes 1179664 | tf_op jit(solution)/shard_map/all_gather | solution.py:103
  244.4 27.2 %all-gather.12.cloned.1.call-done = bf16[512,1536]{1,0:T(8,128)(2,1)} async-done(((bf16[512,384]{1,0:T(8,128)(2,1)}), bf16[512,1536]{1,0:T(8,128)(2,1)}) %all-gather.12.cloned.1.call-update) | async-done | bytes 1572880 | tf_op jit(solution)/shard_map/all_gather | solution.py:118
  271.6 8.2 multiply_reduce_fusion.1
  279.8 0.7 multiply_multiply_fusion.7
  280.7 0.6 multiply_convert_fusion.2
  281.3 0.2 multiply_convert_fusion.1
  281.6 3.8 fusion.12
  285.4 8.2 copy.19
  293.6 0.6 copy-done.27
  294.2 2.6 convolution_convert_fusion.1
  296.8 1.6 copy.20
  298.5 4.4 convolution_convert_fusion
  303.0 0.3 reduce-scatter.9.cloned.1.call-start
  303.3 3.9 fusion.46
  307.3 0.6 copy-done.28
  307.9 0.6 dynamic-slice
  309.3 1.2 stack.39
  310.6 181.5 %all-reduce.20.cloned.1.call-done = f32[1536,2,384]{2,1,0:T(2,128)} async-done(((f32[1536,2,384]{2,1,0:T(2,128)}), f32[1536,2,384]{2,1,0:T(2,128)}) %all-reduce.20.cloned.1.call-update) | async-done | bytes 4718608
  492.1 1.6 dynamic-slice_multiply_fusion
  493.6 26.4 %reduce-scatter.7.cloned.1.call-done = bf16[384,512]{1,0:T(8,128)(2,1)} async-done(((bf16[1536,512]{1,0:T(8,128)(2,1)}), bf16[384,512]{1,0:T(8,128)(2,1)}) %reduce-scatter.7.cloned.1.call-update) | async-done | bytes 393232
  520.0 1.2 copy.21
  521.2 69.5 %all-gather.16.cloned.1.call-done = bf16[2048,1536]{1,0:T(8,128)(2,1)} async-done(((bf16[512,1536]{1,0:T(8,128)(2,1)}), bf16[2048,1536]{1,0:T(8,128)(2,1)}) %all-gather.16.cloned.1.call-update) | async-done | bytes 6291472 | tf_op jit(solution)/shard_map/all_gather | solution.py:13
  590.7 4.7 reduce_sum.150
  595.5 0.4 convert_element_type.112
  595.9 0.3 copy-done.10
  596.2 1.1 fusion.11
  597.2 0.4 multiply_reduce_fusion.10
  597.7 2.6 gather_fusion.3
  600.3 10.5 %all-to-all-start.2 = ((bf16[64,8,384]{2,1,0:T(8,128)(2,1)}), bf16[64,8,384]{2,1,0:T(8,128)(2,1)S(1)}, u32[]{:S(2)}, u32[]{:S(2)}) async-start(bf16[64,8,384]{2,1,0:T(8,128)(2,1)} %bitcast.8), calls=%async_computation.2 | async-start | bytes 786432 | tf_op jit(solution)/shard_map/all_to_all | solution.py:162
  610.7 0.8 add_convert_fusion
  611.6 119.0 %reduce-scatter.9.cloned.1.call-done = f32[384,24]{0,1:T(8,128)} async-done(((f32[384,1536]{0,1:T(8,128)}), f32[384,24]{0,1:T(8,128)}) %reduce-scatter.9.cloned.1.call-update) | async-done | bytes 36880
  730.6 1.4 broadcast_multiply_fusion.2
  732.0 246.1 %all-reduce.17 = (f32[384]{0:T(512)S(1)}, f32[9,384]{1,0:T(8,128)S(1)}) all-reduce(f32[384]{0:T(512)S(1)} %get-tuple-element.30, f32[9,384]{1,0:T(8,128)S(1)} %copy-done.8), channel_id=1, replica_groups=mesh['dp'=64,'seq'=4] {'dp'}, use_global_device_ids=true, to_apply=%region_12.13 | all-reduce | flops 3840 | bytes 30720 | tf_op jit(solution)/shard_map/psum | solution.py:158
  978.1 0.6 broadcast_multiply_fusion.4
  978.7 0.6 broadcast_multiply_fusion.3
  979.4 2.6 gather_fusion.4
  (104 shorter events, 2.1 us)
Async XLA Ops:
  7.2 22.1 %copy-start.6 = (bf16[512,384]{1,0:T(8,128)(2,1)S(1)}, bf16[512,384]{1,0:T(8,128)(2,1)}, u32[]{:S(2)}) copy-start(bf16[512,384]{1,0:T(8,128)(2,1)} %param.8) | copy-start | bytes 1179652
  10.9 3.2 copy-start.11
  17.1 21.6 %all-to-all-start.1 = ((s32[64,1,8]{2,1,0:T(1,128)}), s32[64,1,8]{2,1,0:T(1,128)S(1)}, u32[]{:S(2)}, u32[]{:S(2)}) async-start(s32[64,1,8]{2,1,0:T(1,128)} %bitcast.4), calls=%async_computation.1 | async-start | bytes 65536 | tf_op jit(solution)/shard_map/all_to_all | solution.py:91
  38.7 19.1 %all-to-all-start = ((bf16[64,8,384]{2,1,0:T(8,128)(2,1)}), bf16[64,8,384]{2,1,0:T(8,128)(2,1)S(1)}, u32[]{:S(2)}, u32[]{:S(2)}) async-start(bf16[64,8,384]{2,1,0:T(8,128)(2,1)} %bitcast.2), calls=%async_computation | async-start | bytes 786432 | tf_op jit(solution)/shard_map/all_to_all | solution.py:90
  43.3 42.2 %all-gather.14.cloned.1.call-start = ((), (), s32[]{:S(2)}) async-start(), calls=%async_computation.8 | async-start | bytes 1966080 | tf_op jit(solution)/shard_map/all_gather | solution.py:94
  44.7 13.1 %copy-start.13 = (s32[512,1]{0,1:T(1,128)}, s32[512,1]{0,1:T(1,128)S(1)}, u32[]{:S(2)}) copy-start(s32[512,1]{0,1:T(1,128)S(1)} %compare_select_fusion) | copy-start | bytes 6148
  57.9 4.9 copy-start.15
  57.9 5.0 copy-start.16
  60.5 106.8 %all-gather.8.cloned.1.call-start = ((), (), s32[]{:S(2)}) async-start(), calls=%async_computation.5 | async-start | bytes 2396160 | tf_op jit(solution)/shard_map/all_gather | solution.py:102
  61.3 183.1 %all-gather.10.cloned.1.call-start = ((), (), s32[]{:S(2)}) async-start(), calls=%async_computation.6 | async-start | bytes 1198080 | tf_op jit(solution)/shard_map/all_gather | solution.py:103
  62.0 209.6 %all-gather.12.cloned.1.call-start = ((), (), s32[]{:S(2)}) async-start(), calls=%async_computation.7 | async-start | bytes 1966080 | tf_op jit(solution)/shard_map/all_gather | solution.py:118
  62.6 429.5 %all-reduce.20.cloned.1.call-start = ((), (), s32[]{:S(2)}) async-start(), calls=%async_computation.11 | async-start | bytes 9437184
  63.0 208.7 %copy-start.26 = (f32[512]{0:T(512)}, f32[512]{0:T(512)S(1)}, u32[]{:S(2)}) copy-start(f32[512]{0:T(512)S(1)} %compare_convert_fusion) | copy-start | bytes 6148
  85.6 1.9 copy-start
  167.3 2.2 copy-start.9
  169.5 1.5 copy-start.3
  171.2 0.9 copy-start.2
  281.6 3.8 copy-start.7
  293.6 0.7 copy-start.27
  293.6 226.4 %reduce-scatter.7.cloned.1.call-start = ((), (), s32[]{:S(2)}) async-start(), calls=%async_computation.10 | async-start | bytes 1966080
  298.5 4.8 copy-start.5
  298.5 292.3 %all-gather.16.cloned.1.call-start = ((), (), s32[]{:S(2)}) async-start(), calls=%async_computation.9 | async-start | bytes 7864320 | tf_op jit(solution)/shard_map/all_gather | solution.py:13
  303.0 427.6 %reduce-scatter.9.cloned.1.call-start = ((), (), s32[]{:S(2)}) async-start(), calls=%async_computation.12 | async-start | bytes 2396160
  307.2 0.7 copy-start.28
  307.2 1.9 copy-start.12
  307.2 1.9 copy-start.14
  307.2 2.0 copy-start.25
  307.2 2.0 copy-start.24
  307.2 2.0 copy-start.23
  307.2 2.0 copy-start.22
  307.2 2.0 copy-start.21
  307.2 2.0 copy-start.20
  307.3 2.0 copy-start.19
  307.3 2.0 copy-start.18
  307.3 2.0 copy-start.17
  595.5 0.7 copy-start.10
  596.2 1.1 copy-start.4
  597.7 13.1 %copy-start.1 = (bf16[512,384]{1,0:T(8,128)(2,1)S(1)}, bf16[512,384]{1,0:T(8,128)(2,1)}, u32[]{:S(2)}) copy-start(bf16[512,384]{1,0:T(8,128)(2,1)} %gather_fusion.2) | copy-start | bytes 1179652
  597.7 134.3 %copy-start.8 = (f32[9,384]{1,0:T(8,128)S(1)}, f32[9,384]{1,0:T(8,128)}, u32[]{:S(2)}) copy-start(f32[9,384]{1,0:T(8,128)} %stack.39) | copy-start | bytes 41476
  600.3 379.1 %all-to-all-start.2 = ((bf16[64,8,384]{2,1,0:T(8,128)(2,1)}), bf16[64,8,384]{2,1,0:T(8,128)(2,1)S(1)}, u32[]{:S(2)}, u32[]{:S(2)}) async-start(bf16[64,8,384]{2,1,0:T(8,128)(2,1)} %bitcast.8), calls=%async_computation.2 | async-start | bytes 786432 | tf_op jit(solution)/shard_map/all_to_all | solution.py:162
Sparse Core Ops, SparseCore 0:
  60.6 24.8 all-gather.13
  88.2 79.0 all-gather.7
  170.0 74.3 all-gather.9
  246.1 25.4 all-gather.11
  293.7 198.3 all-reduce.19
  494.5 25.4 reduce-scatter.6
  521.8 68.8 all-gather.15
  594.9 135.6 reduce-scatter.8
